TPU v7x, 512 devices: a whole 4x4x16 slice. The times are simulated.
512 devices in a mesh: mpo: 8 (over y, core), sec: 64 (over x, z).
Axes of the slice: x: 4, y: 4, z: 16, core: 2. Of those that a mesh axis runs over, the one named last changes fastest.
Arguments:
- theta: bfloat16 [16, 1024, 1024], P(None, 'sec'), may hold values from -6 to 6
- env_left: bfloat16 [24, 16384, 1024], P('mpo', 'sec'), may hold values from -0.1875 to 0.1875
- env_right: bfloat16 [24, 16384, 1024], P('mpo', 'sec'), may hold values from -0.0390625 to 0.0390625
- mpo_core: float32 [24, 24], replicated, may hold values from -1.25 to 1.25
- sector_sizes: int32 [16], replicated, may hold values from 1 to 1024, 12288 in all
Outputs:
- applied: bfloat16 [1024, 16384], P('mpo', 'sec')
Inputs may be any that keep to these rules, and one draw needn't show every extreme that they name: `sector_sizes`: one sector has exactly 1024 states in use; the sizes sum to 12288.
All inputs are finite; a program needn't handle non-finite values.
Results may differ from a plain program's by a relative error of at most 0.0058.
Values may be sent and summed in bfloat16 or wider, within the bound.
No kernel may reach another device: no remote copies, remote signals or barrier semaphores. Data moves between devices by JAX's collectives and lax.ppermute only.
A program may use at most 64 MiB of HBM per device.

v0:
```python
import jax
import jax.numpy as jnp
from jax import lax
from jax.sharding import PartitionSpec as P

G = 4


def swapped(array, axis, stride):
    return lax.ppermute(array, axis, [(i, i ^ 1 << stride) for i in range(lax.axis_size(axis))])


def on_device(theta, env_left, env_right, mpo_core, sector_sizes):
    sectors = theta.shape[0]
    rows_local = theta.shape[1]
    width = theta.shape[2]
    local_w = env_left.shape[0]
    slab = env_left.shape[1]
    sec_place = lax.axis_index("sec")
    sector = sec_place // G
    block_pos = sec_place % G
    live_size = jnp.sum(jnp.where(jnp.arange(sectors, dtype=jnp.int32) == sector, sector_sizes, 0))
    bit_count = G.bit_length() - 1
    spread = jnp.broadcast_to(theta[:, None], (sectors, G, rows_local, width))
    spread = spread.reshape(sectors * G, rows_local, width)
    sector_block = lax.all_to_all(spread, "sec", split_axis=0, concat_axis=1, tiled=True)[0]
    positions = jnp.arange(width, dtype=jnp.int32)
    keep_row = positions < live_size
    sector_block = jnp.where(
        keep_row[:, None] & keep_row[None, :], sector_block, jnp.zeros_like(sector_block)
    )
    product = jnp.einsum(
        "akm,mn->akn", env_left, sector_block, preferred_element_type=jnp.float32
    ).astype(jnp.bfloat16)
    own_start = lax.axis_index("mpo") * local_w
    core_cols = lax.dynamic_slice_in_dim(mpo_core, own_start, local_w, 1)
    mixed = jnp.einsum(
        "ab,akn->bkn",
        core_cols,
        lax.all_gather(product, "mpo", axis=0, tiled=True).astype(jnp.float32),
        precision=lax.Precision.HIGHEST,
    ).astype(jnp.bfloat16)
    for bit_index in range(bit_count):
        partner = swapped(mixed, "sec", bit_index)
        upper_half = sec_place >> bit_index & 1 == 1
        mixed = jnp.where(
            upper_half, jnp.concatenate([partner, mixed], 1), jnp.concatenate([mixed, partner], 1)
        )
    col_keep = block_pos * slab + jnp.arange(slab, dtype=jnp.int32) < live_size
    sector_term = jnp.einsum("bil,bjl->ij", mixed, env_right, preferred_element_type=jnp.float32)
    row_keep = (
        jnp.arange(lax.axis_size("mpo") * (width // lax.axis_size("mpo")), dtype=jnp.int32)
        < live_size
    )
    result = lax.psum_scatter(
        jnp.where(row_keep[:, None] & col_keep[None, :], sector_term, jnp.zeros_like(sector_term)),
        "mpo",
        scatter_dimension=0,
        tiled=True,
    )
    return result.astype(jnp.bfloat16)


def solution(mesh):
    return jax.shard_map(
        on_device,
        mesh=mesh,
        in_specs=(P(None, "sec", None), P("mpo", "sec", None), P("mpo", "sec", None), P(), P()),
        out_specs=P("mpo", "sec"),
        check_vma=False,
    )
```

profile of v0, /device:TPU:2, one launch (start us, length us, event | category | flops | bytes accessed | tf_op | source)
XLA Modules:
  0.0 477.4 jit_solution(1534336615428155424)
XLA Ops:
  6.5 0.0 copy-start
  6.5 0.0 copy-start.7
  6.5 2.8 broadcast_in_dim.11
  9.3 18.8 %all-to-all-start = ((bf16[64,16,1024]{2,1,0:T(8,128)(2,1)}), bf16[64,16,1024]{2,1,0:T(8,128)(2,1)}, u32[]{:S(2)}, u32[]{:S(2)}) async-start(bf16[64,16,1024]{2,1,0:T(8,128)(2,1)} %bitcast.21), calls=%async_computation | async-start | bytes 4194304 | tf_op jit(solution)/shard_map/all_to_all | solution.py:26
  28.1 0.0 all-gather.2.cloned.1.call-start
  28.2 0.0 copy-done.7
  28.2 0.6 fusion.27
  28.8 0.6 iota_compare_fusion
  29.5 95.7 %all-to-all-done = bf16[64,16,1024]{2,1,0:T(8,128)(2,1)} async-done(((bf16[64,16,1024]{2,1,0:T(8,128)(2,1)}), bf16[64,16,1024]{2,1,0:T(8,128)(2,1)}, u32[]{:S(2)}, u32[]{:S(2)}) %all-to-all-start) | async-done | bytes 2097184 | tf_op jit(solution)/shard_map/all_to_all | solution.py:26
  125.2 0.0 copy-done
  125.2 0.0 copy-start.5
  125.2 4.9 %fusion.15 = bf16[3,256,1024]{2,1,0:T(8,128)(2,1)} fusion(bf16[3,256,1024]{2,1,0:T(8,128)(2,1)S(1)} %copy-done, bf16[1024,1024]{1,0:T(8,128)(2,1)} %bitcast.2, pred[1024]{0:T(1024)(128)(4,1)S(1)} %iota_compare_fusion), kind=kOutput, calls=%fused_computation.13 | convolution fusion | flops 1613496320 | bytes 5243904 | tf_op jit(solution)/shard_map/akm,mn->akn/dot_general | solution.py:32
  130.1 0.0 all-gather.2.cloned.1.call-update
  130.1 0.0 reduce-scatter.2.cloned.1.call-start
  130.2 69.3 %all-gather.2.cloned.1.call-done = bf16[24,256,1024]{2,1,0:T(8,128)(2,1)} async-done(((bf16[3,256,1024]{2,1,0:T(8,128)(2,1)}), bf16[24,256,1024]{2,1,0:T(8,128)(2,1)}) %all-gather.2.cloned.1.call-update) | async-done | bytes 12582928 | tf_op jit(solution)/shard_map/all_gather | solution.py:40
  199.5 0.0 copy-done.5
  199.5 17.3 %fusion.9 = bf16[3,256,1024]{2,0,1:T(4,128)(2,1)S(1)} fusion(bf16[24,256,1024]{2,1,0:T(8,128)(2,1)} %all-gather.2.cloned.1.call-done, f32[24,24]{1,0:T(8,128)S(1)} %copy-done.5, s32[]{:T(128)S(6)} %select_n.47), kind=kOutput, calls=%fused_computation.11 | convolution fusion | flops 227278848 | bytes 14158084 | tf_op jit(solution)/shard_map/ab,akn->bkn/dot_general | solution.py:37
  216.8 0.0 copy-start.3
  216.8 1.3 copy-done.3
  218.1 1.8 copy.10
  219.8 3.6 collective-permute-start
  223.5 0.0 copy-start.4
  223.5 35.0 %collective-permute-done = bf16[3,256,1024]{2,1,0:T(8,128)(2,1)S(1)} collective-permute-done((bf16[3,256,1024]{2,1,0:T(8,128)(2,1)}, bf16[3,256,1024]{2,1,0:T(8,128)(2,1)S(1)}, u32[]{:S(2)}, u32[]{:S(2)}) %collective-permute-start) | collective-permute-done | bytes 1572896 | tf_op jit(solution)/shard_map/ppermute | solution.py:10
  258.5 1.4 copy.11
  259.8 0.0 copy-done.4
  259.9 4.7 maximum_select_fusion.1
  264.5 0.0 copy-start.1
  264.5 1.9 copy-done.1
  266.5 2.9 copy.13
  269.4 4.4 collective-permute-start.1
  273.9 0.0 copy-start.2
  273.9 0.8 add_compare_fusion
  274.7 134.6 %collective-permute-done.1 = bf16[3,512,1024]{2,1,0:T(8,128)(2,1)} collective-permute-done((bf16[3,512,1024]{2,1,0:T(8,128)(2,1)}, bf16[3,512,1024]{2,1,0:T(8,128)(2,1)}, u32[]{:S(2)}, u32[]{:S(2)}) %collective-permute-start.1) | collective-permute-done | bytes 3145760 | tf_op jit(solution)/shard_map/ppermute | solution.py:10
  409.3 4.6 copy.14
  413.9 0.0 copy-done.2
  413.9 0.0 copy-start.6
  413.9 9.3 %maximum_select_fusion = bf16[3,1024,1024]{2,0,1:T(4,128)(2,1)S(1)} fusion(bf16[3,512,1024]{2,0,1:T(4,128)(2,1)S(1)} %copy-done.2, bf16[3,512,1024]{2,0,1:T(4,128)(2,1)S(1)} %copy.14, pred[]{:T(512)S(6)} %eq.16), kind=kLoop, calls=%fused_computation.2 | loop fusion | flops 9437184 | bytes 12582913 | tf_op jit(solution)/shard_map/jit(_where)/select_n | solution.py:46
  423.3 0.0 copy-done.6
  423.3 5.2 %fusion.21 = f32[1024,256]{1,0:T(8,128)} fusion(bf16[3,256,1024]{2,1,0:T(8,128)(2,1)S(1)} %copy-done.6, bf16[3,1024,1024]{2,0,1:T(4,128)(2,1)S(1)} %maximum_select_fusion, pred[256]{0:T(512)(128)(4,1)S(1)} %add_compare_fusion, pred[1024]{0:T(1024)(128)(4,1)S(1)} %iota_compare_fusion), kind=kOutput, calls=%fused_computation.15 | convolution fusion | flops 1611137024 | bytes 8914176 | tf_op jit(solution)/shard_map/bil,bjl->ij/dot_general | solution.py:50
  428.5 0.0 reduce-scatter.2.cloned.1.call-update
  428.5 40.5 %reduce-scatter.2.cloned.1.call-done = f32[128,256]{1,0:T(8,128)} async-done(((f32[1024,256]{1,0:T(8,128)}), f32[128,256]{1,0:T(8,128)}) %reduce-scatter.2.cloned.1.call-update) | async-done | bytes 131088 | tf_op jit(solution)/shard_map/reduce_scatter | solution.py:55
  469.0 1.5 convert_element_type.16
Async XLA Ops:
  6.5 118.7 %copy-start = (bf16[3,256,1024]{2,1,0:T(8,128)(2,1)S(1)}, bf16[3,256,1024]{2,1,0:T(8,128)(2,1)}, u32[]{:S(2)}) copy-start(bf16[3,256,1024]{2,1,0:T(8,128)(2,1)} %param.6) | copy-start | bytes 4718596
  6.5 21.7 %copy-start.7 = (s32[16]{0:T(128)S(1)}, s32[16]{0:T(128)}, u32[]{:S(2)}) copy-start(s32[16]{0:T(128)} %param.9) | copy-start | bytes 196
  9.3 115.9 %all-to-all-start = ((bf16[64,16,1024]{2,1,0:T(8,128)(2,1)}), bf16[64,16,1024]{2,1,0:T(8,128)(2,1)}, u32[]{:S(2)}, u32[]{:S(2)}) async-start(bf16[64,16,1024]{2,1,0:T(8,128)(2,1)} %bitcast.21), calls=%async_computation | async-start | bytes 4194304 | tf_op jit(solution)/shard_map/all_to_all | solution.py:26
  28.1 171.4 %all-gather.2.cloned.1.call-start = ((), (), s32[]{:S(2)}) async-start(), calls=%async_computation.2 | async-start | bytes 14155776 | tf_op jit(solution)/shard_map/all_gather | solution.py:40
  125.2 74.3 %copy-start.5 = (f32[24,24]{1,0:T(8,128)S(1)}, f32[24,24]{1,0:T(8,128)}, u32[]{:S(2)}) copy-start(f32[24,24]{1,0:T(8,128)} %param.8) | copy-start | bytes 6916
  130.1 338.9 %reduce-scatter.2.cloned.1.call-start = ((), (), s32[]{:S(2)}) async-start(), calls=%async_computation.3 | async-start | bytes 1179648 | tf_op jit(solution)/shard_map/reduce_scatter | solution.py:55
  216.8 1.3 copy-start.3
  219.8 38.6 %collective-permute-start = (bf16[3,256,1024]{2,1,0:T(8,128)(2,1)}, bf16[3,256,1024]{2,1,0:T(8,128)(2,1)S(1)}, u32[]{:S(2)}, u32[]{:S(2)}) collective-permute-start(bf16[3,256,1024]{2,1,0:T(8,128)(2,1)} %copy.10), channel_id=1, source_target_pairs={{0,1},{1,0},{2,3},{3,2},{4,5},{5,4},{6,7},{7,6},{8,9},{9,8},{10,11... | collective-permute-start | bytes 4718600 | tf_op jit(solution)/shard_map/ppermute | solution.py:10
  223.5 36.4 %copy-start.4 = (bf16[3,256,1024]{2,0,1:T(4,128)(2,1)S(1)}, bf16[3,256,1024]{2,0,1:T(4,128)(2,1)}, u32[]{:S(2)}) copy-start(bf16[3,256,1024]{2,0,1:T(4,128)(2,1)} %copy-done.3) | copy-start | bytes 4718596
  264.5 2.0 copy-start.1
  269.4 139.9 %collective-permute-start.1 = (bf16[3,512,1024]{2,1,0:T(8,128)(2,1)}, bf16[3,512,1024]{2,1,0:T(8,128)(2,1)}, u32[]{:S(2)}, u32[]{:S(2)}) collective-permute-start(bf16[3,512,1024]{2,1,0:T(8,128)(2,1)} %copy.13), channel_id=1, source_target_pairs={{0,2},{1,3},{2,0},{3,1},{4,6},{5,7},{6,4},{7,5},{8,10},{9,11},{10,... | collective-permute-start | bytes 9437192 | tf_op jit(solution)/shard_map/ppermute | solution.py:10
  273.9 140.0 %copy-start.2 = (bf16[3,512,1024]{2,0,1:T(4,128)(2,1)S(1)}, bf16[3,512,1024]{2,0,1:T(4,128)(2,1)}, u32[]{:S(2)}) copy-start(bf16[3,512,1024]{2,0,1:T(4,128)(2,1)} %copy-done.1) | copy-start | bytes 9437188
  413.9 9.3 %copy-start.6 = (bf16[3,256,1024]{2,1,0:T(8,128)(2,1)S(1)}, bf16[3,256,1024]{2,1,0:T(8,128)(2,1)}, u32[]{:S(2)}) copy-start(bf16[3,256,1024]{2,1,0:T(8,128)(2,1)} %param.7) | copy-start | bytes 4718596
Sparse Core Ops, SparseCore 0:
  130.3 69.1 all-gather.1
  428.7 40.3 reduce-scatter.1
where the time goes:
time: 478 us; the launch traced here: 477 us
  waiting for transfers between devices  375 us (78%)
  matrix products  27.4 us (6%)
  starting transfers between devices  27 us (6%)
  other arithmetic  17.6 us (4%)
  local copies, waits for them, and re-layouts  16.7 us (3%)
  between operations  13.6 us (3%)
    ppermute x2, waiting for transfers between devices, swapped(): lax.ppermute(array, axis, [(i, i ^ 1 << stride) for i in range(lax.axis_s...  170 us
    all_to_all x1, waiting for transfers between devices, on_device(): lax.all_to_all(spread, 'sec', split_axis=0, concat_axis=1, tiled=True)[0]  95.7 us
    all_gather x1, waiting for transfers between devices, on_device(): lax.all_gather(product, 'mpo', axis=0, tiled=True).astype(jnp.float32)  69.3 us
    reduce_scatter x1, waiting for transfers between devices, on_device(): lax.psum_scatter(jnp.where(row_keep[:, None] & col_keep[None, :], sector_...  40.5 us
    all_to_all x1, starting transfers between devices, on_device(): lax.all_to_all(spread, 'sec', split_axis=0, concat_axis=1, tiled=True)[0]  18.8 us
    dot_general x1, matrix products, on_device(): jnp.einsum('ab,akn->bkn', core_cols, lax.all_gather(product, 'mpo', axis=...  17.3 us
    select_n x2, other arithmetic, on_device(): jnp.where(upper_half, jnp.concatenate([partner, mixed], 1), jnp.concatena...  14 us
  transfers between devices with their start and end apart: 5, of which 5 were waited for; matrix products, arithmetic and copies ran while one was open for 0% of the time, Pallas kernels for 0%

commit v1 on v0

--- a/solution.py
+++ b/solution.py
@@ -4,6 +4,19 @@
 from jax.sharding import PartitionSpec as P
 
 G = 4
+
+
+def gather_around(x, axis, dim):
+    ways = lax.axis_size(axis)
+    up = [(d, (d + 1) % ways) for d in range(ways)]
+    down = [(d, (d - 1) % ways) for d in range(ways)]
+    earlier, later = ([x], [x])
+    for _ in range(ways // 2):
+        earlier.append(lax.ppermute(earlier[-1], axis, up))
+    for _ in range((ways - 1) // 2):
+        later.append(lax.ppermute(later[-1], axis, down))
+    line = jnp.concatenate([*earlier[::-1], *later[1:]], axis=dim)
+    return jnp.roll(line, (lax.axis_index(axis) - ways // 2) * x.shape[dim], axis=dim)
 
 
 def swapped(array, axis, stride):
@@ -37,7 +50,7 @@
     mixed = jnp.einsum(
         "ab,akn->bkn",
         core_cols,
-        lax.all_gather(product, "mpo", axis=0, tiled=True).astype(jnp.float32),
+        gather_around(product, "mpo", 0).astype(jnp.float32),
         precision=lax.Precision.HIGHEST,
     ).astype(jnp.bfloat16)
     for bit_index in range(bit_count):

time: 478 us -> 509 us (1.065)
  the two profiles are of different devices: /device:TPU:2 before, /device:TPU:4 now
where the time goes in v1:
time: 509 us; the launch traced here: 508 us
  waiting for transfers between devices  369 us (72%)
  local copies, waits for them, and re-layouts  51.3 us (10%)
  starting transfers between devices  36.7 us (7%)
  other arithmetic  19 us (4%)
  matrix products  17.8 us (3%)
  between operations  13.7 us (3%)
    ppermute x2, waiting for transfers between devices, swapped(): lax.ppermute(array, axis, [(i, i ^ 1 << stride) for i in range(lax.axis_s...  158 us
    all_to_all x1, waiting for transfers between devices, on_device(): lax.all_to_all(spread, 'sec', split_axis=0, concat_axis=1, tiled=True)[0]  95.9 us
    ppermute x4, waiting for transfers between devices, gather_around(): earlier.append(lax.ppermute(earlier[-1], axis, up))  73.4 us
    reduce_scatter x1, waiting for transfers between devices, on_device(): lax.psum_scatter(jnp.where(row_keep[:, None] & col_keep[None, :], sector_...  41.2 us
    dynamic_slice x2, local copies, waits for them, and re-layouts, gather_around(): jnp.roll(line, (lax.axis_index(axis) - ways // 2) * x.shape[dim], axis=dim)  21.5 us
    all_to_all x1, starting transfers between devices, on_device(): lax.all_to_all(spread, 'sec', split_axis=0, concat_axis=1, tiled=True)[0]  18.9 us
    unnamed x39, local copies, waits for them, and re-layouts  16 us
    select_n x2, other arithmetic, on_device(): jnp.where(upper_half, jnp.concatenate([partner, mixed], 1), jnp.concatena...  15.3 us
  transfers between devices with their start and end apart: 11, of which 9 were waited for; matrix products, arithmetic and copies ran while one was open for 1% of the time, Pallas kernels for 0%

profile of v1, /device:TPU:4, one launch (start us, length us, event | category | flops | bytes accessed | tf_op | source)
XLA Modules:
  0.0 507.8 jit_solution(12060296069272991342)
XLA Ops:
  6.5 0.0 copy-start
  6.5 2.8 broadcast_in_dim.11
  9.3 18.9 %all-to-all-start = ((bf16[64,16,1024]{2,1,0:T(8,128)(2,1)}), bf16[64,16,1024]{2,1,0:T(8,128)(2,1)}, u32[]{:S(2)}, u32[]{:S(2)}) async-start(bf16[64,16,1024]{2,1,0:T(8,128)(2,1)} %bitcast.22), calls=%async_computation | async-start | bytes 4194304 | tf_op jit(solution)/shard_map/all_to_all | solution.py:39
  28.2 0.0 reduce-scatter.2.cloned.1.call-start
  28.3 0.0 copy-done.11
  28.3 0.6 fusion.22
  28.9 0.6 iota_compare_fusion
  29.6 95.9 %all-to-all-done = bf16[64,16,1024]{2,1,0:T(8,128)(2,1)} async-done(((bf16[64,16,1024]{2,1,0:T(8,128)(2,1)}), bf16[64,16,1024]{2,1,0:T(8,128)(2,1)}, u32[]{:S(2)}, u32[]{:S(2)}) %all-to-all-start) | async-done | bytes 2097184 | tf_op jit(solution)/shard_map/all_to_all | solution.py:39
  125.5 0.0 copy-done
  125.5 3.6 fusion.10
  129.1 0.0 collective-permute-start
  129.1 21.0 %collective-permute-done = bf16[3,256,1024]{1,2,0:T(8,128)(2,1)S(1)} collective-permute-done((bf16[3,256,1024]{1,2,0:T(8,128)(2,1)S(1)}, bf16[3,256,1024]{1,2,0:T(8,128)(2,1)S(1)}, u32[]{:S(2)}, u32[]{:S(2)}) %collective-permute-start) | collective-permute-done | bytes 1572896 | tf_op jit(solution)/shard_map/ppermute | solution.py:15
  150.2 0.0 collective-permute-start.1
  150.2 3.0 collective-permute-start.4
  153.1 18.1 %collective-permute-done.1 = bf16[3,256,1024]{1,2,0:T(8,128)(2,1)S(1)} collective-permute-done((bf16[3,256,1024]{1,2,0:T(8,128)(2,1)S(1)}, bf16[3,256,1024]{1,2,0:T(8,128)(2,1)S(1)}, u32[]{:S(2)}, u32[]{:S(2)}) %collective-permute-start.1) | collective-permute-done | bytes 1572896 | tf_op jit(solution)/shard_map/ppermute | solution.py:15
  171.2 0.0 collective-permute-start.2
  171.2 0.0 collective-permute-done.4
  171.2 1.2 copy-done.5
  172.4 2.9 collective-permute-start.5
  175.3 17.0 %collective-permute-done.2 = bf16[3,256,1024]{1,2,0:T(8,128)(2,1)} collective-permute-done((bf16[3,256,1024]{1,2,0:T(8,128)(2,1)S(1)}, bf16[3,256,1024]{1,2,0:T(8,128)(2,1)}, u32[]{:S(2)}, u32[]{:S(2)}) %collective-permute-start.2) | collective-permute-done | bytes 1572896 | tf_op jit(solution)/shard_map/ppermute | solution.py:15
  192.4 0.0 collective-permute-start.3
  192.4 0.9 collective-permute-done.5
  193.3 3.2 collective-permute-start.6
  196.5 17.3 %collective-permute-done.3 = bf16[3,256,1024]{1,2,0:T(8,128)(2,1)} collective-permute-done((bf16[3,256,1024]{1,2,0:T(8,128)(2,1)}, bf16[3,256,1024]{1,2,0:T(8,128)(2,1)}, u32[]{:S(2)}, u32[]{:S(2)}) %collective-permute-start.3) | collective-permute-done | bytes 1572896 | tf_op jit(solution)/shard_map/ppermute | solution.py:15
  213.8 1.5 constant_dynamic-update-slice_fusion.15
  215.3 1.6 constant_dynamic-update-slice_fusion.14
  216.9 0.1 constant_dynamic-update-slice_fusion.13
  217.0 0.1 constant_dynamic-update-slice_fusion.12
  217.1 0.1 constant_dynamic-update-slice_fusion.11
  217.3 0.1 constant_dynamic-update-slice_fusion.10
  217.4 1.5 constant_dynamic-update-slice_fusion.9
  218.9 0.0 collective-permute-done.6
  218.9 1.5 constant_dynamic-update-slice_fusion.8
  220.4 1.5 constant_dynamic-update-slice_fusion.7
  221.9 1.5 constant_dynamic-update-slice_fusion.6
  223.4 0.1 constant_dynamic-update-slice_fusion.5
  223.6 0.1 constant_dynamic-update-slice_fusion.4
  223.7 0.1 constant_dynamic-update-slice_fusion.3
  223.8 0.1 constant_dynamic-update-slice_fusion.2
  223.9 1.5 constant_dynamic-update-slice_fusion.1
  225.4 1.5 constant_dynamic-update-slice_fusion
  226.9 5.1 %constant_dynamic-slice_fusion = bf16[24,256,1024]{1,2,0:T(8,128)(2,1)} fusion(bf16[48,256,1024]{1,2,0:T(8,128)(2,1)S(1)} %constant_dynamic-update-slice_fusion, s32[]{:T(128)S(6)} %select_n.62), kind=kLoop, calls=%fused_computation.37 | loop fusion | bytes 25165828 | tf_op jit(solution)/shard_map/jit(_roll_dynamic)/dynamic_slice | solution.py:19
  232.0 16.4 %copy.16 = bf16[24,256,1024]{2,0,1:T(8,128)(2,1)} copy(bf16[24,256,1024]{1,2,0:T(8,128)(2,1)} %constant_dynamic-slice_fusion) | data formatting | bytes 25165824 | tf_op jit(solution)/shard_map/jit(_roll_dynamic)/dynamic_slice | solution.py:19
  248.5 8.9 %convolution_convert_fusion = bf16[3,256,1024]{2,0,1:T(4,128)(2,1)S(1)} fusion(bf16[24,256,1024]{2,0,1:T(8,128)(2,1)} %copy.16, f32[24,24]{1,0:T(8,128)S(1)} %copy-done.9, s32[]{:T(128)S(6)} %select_n.59), kind=kOutput, calls=%fused_computation.9 | convolution fusion | flops 227278848 | bytes 14158084 | tf_op jit(solution)/shard_map/ab,akn->bkn/dot_general | solution.py:50
  257.4 1.3 copy-done.4
  258.7 0.6 copy.17
  259.3 4.4 collective-permute-start.7
  263.7 28.7 %collective-permute-done.7 = bf16[3,256,1024]{2,1,0:T(8,128)(2,1)S(1)} collective-permute-done((bf16[3,256,1024]{2,1,0:T(8,128)(2,1)S(1)}, bf16[3,256,1024]{2,1,0:T(8,128)(2,1)S(1)}, u32[]{:S(2)}, u32[]{:S(2)}) %collective-permute-start.7) | collective-permute-done | bytes 1572896 | tf_op jit(solution)/shard_map/ppermute | solution.py:23
  292.4 1.4 copy.18
  293.8 6.0 %maximum_select_fusion.1 = bf16[3,512,1024]{2,0,1:T(4,128)(2,1)S(1)} fusion(bf16[3,256,1024]{2,0,1:T(4,128)(2,1)} %copy-done.4, bf16[3,256,1024]{2,0,1:T(4,128)(2,1)S(1)} %copy.18, pred[]{:T(512)S(6)} %eq.20), kind=kLoop, calls=%fused_computation.3 | loop fusion | flops 4718592 | bytes 6291457 | tf_op jit(solution)/shard_map/jit(_where)/select_n | solution.py:59
  299.8 1.9 copy-done.2
  301.7 2.9 copy.20
  304.7 4.3 collective-permute-start.8
  309.0 0.8 add_compare_fusion
  309.8 129.2 %collective-permute-done.8 = bf16[3,512,1024]{2,1,0:T(8,128)(2,1)} collective-permute-done((bf16[3,512,1024]{2,1,0:T(8,128)(2,1)}, bf16[3,512,1024]{2,1,0:T(8,128)(2,1)}, u32[]{:S(2)}, u32[]{:S(2)}) %collective-permute-start.8) | collective-permute-done | bytes 3145760 | tf_op jit(solution)/shard_map/ppermute | solution.py:23
  439.0 4.6 copy.21
  443.6 0.0 copy-start.10
  443.6 0.0 copy-start.1
  443.6 9.3 %maximum_select_fusion = bf16[3,1024,1024]{2,0,1:T(4,128)(2,1)S(1)} fusion(bf16[3,512,1024]{2,0,1:T(4,128)(2,1)S(1)} %copy-done.3, bf16[3,512,1024]{2,0,1:T(4,128)(2,1)S(1)} %copy.21, pred[]{:T(512)S(6)} %eq.19), kind=kLoop, calls=%fused_computation | loop fusion | flops 9437184 | bytes 12582913 | tf_op jit(solution)/shard_map/jit(_where)/select_n | solution.py:59
  452.9 0.0 copy-done.10
  452.9 5.2 %fusion.16 = f32[1024,256]{1,0:T(8,128)} fusion(bf16[3,256,1024]{2,1,0:T(8,128)(2,1)S(1)} %copy-done.10, bf16[3,1024,1024]{2,0,1:T(4,128)(2,1)S(1)} %maximum_select_fusion, pred[256]{0:T(512)(128)(4,1)S(1)} %add_compare_fusion, pred[1024]{0:T(1024)(128)(4,1)S(1)} %iota_compare_fusion), kind=kOutput, calls=%fused_computation.13 | convolution fusion | flops 1611137024 | bytes 8914176 | tf_op jit(solution)/shard_map/bil,bjl->ij/dot_general | solution.py:63
  458.2 0.0 reduce-scatter.2.cloned.1.call-update
  458.2 41.2 %reduce-scatter.2.cloned.1.call-done = f32[128,256]{1,0:T(8,128)} async-done(((f32[1024,256]{1,0:T(8,128)}), f32[128,256]{1,0:T(8,128)}) %reduce-scatter.2.cloned.1.call-update) | async-done | bytes 131088 | tf_op jit(solution)/shard_map/reduce_scatter | solution.py:68
  499.4 1.5 convert_element_type.16
  (15 shorter events, 0.0 us)
Async XLA Ops:
  6.5 118.9 %copy-start = (bf16[3,256,1024]{2,1,0:T(8,128)(2,1)S(1)}, bf16[3,256,1024]{2,1,0:T(8,128)(2,1)}, u32[]{:S(2)}) copy-start(bf16[3,256,1024]{2,1,0:T(8,128)(2,1)} %param.6) | copy-start | bytes 4718596
  6.5 21.7 %copy-start.11 = (s32[16]{0:T(128)S(1)}, s32[16]{0:T(128)}, u32[]{:S(2)}) copy-start(s32[16]{0:T(128)} %param.9) | copy-start | bytes 196
  9.3 116.2 %all-to-all-start = ((bf16[64,16,1024]{2,1,0:T(8,128)(2,1)}), bf16[64,16,1024]{2,1,0:T(8,128)(2,1)}, u32[]{:S(2)}, u32[]{:S(2)}) async-start(bf16[64,16,1024]{2,1,0:T(8,128)(2,1)} %bitcast.22), calls=%async_computation | async-start | bytes 4194304 | tf_op jit(solution)/shard_map/all_to_all | solution.py:39
  28.2 471.2 %reduce-scatter.2.cloned.1.call-start = ((), (), s32[]{:S(2)}) async-start(), calls=%async_computation.2 | async-start | bytes 1179648 | tf_op jit(solution)/shard_map/reduce_scatter | solution.py:68
  129.1 21.1 %collective-permute-start = (bf16[3,256,1024]{1,2,0:T(8,128)(2,1)S(1)}, bf16[3,256,1024]{1,2,0:T(8,128)(2,1)S(1)}, u32[]{:S(2)}, u32[]{:S(2)}) collective-permute-start(bf16[3,256,1024]{1,2,0:T(8,128)(2,1)S(1)} %fusion.10), channel_id=1, source_target_pairs={{0,64},{64,128},{128,192},{192,256},{256,320},{320,384},{384,448},... | collective-permute-start | bytes 4718600 | tf_op jit(solution)/shard_map/ppermute | solution.py:15
  150.2 21.1 %collective-permute-start.1 = (bf16[3,256,1024]{1,2,0:T(8,128)(2,1)S(1)}, bf16[3,256,1024]{1,2,0:T(8,128)(2,1)S(1)}, u32[]{:S(2)}, u32[]{:S(2)}) collective-permute-start(bf16[3,256,1024]{1,2,0:T(8,128)(2,1)S(1)} %collective-permute-done), channel_id=1, source_target_pairs={{0,64},{64,128},{128,192},{192,256},{256,320},{320,384},{384,448},... | collective-permute-start | bytes 4718600 | tf_op jit(solution)/shard_map/ppermute | solution.py:15
  150.2 21.1 %collective-permute-start.4 = (bf16[3,256,1024]{1,2,0:T(8,128)(2,1)S(1)}, bf16[3,256,1024]{1,2,0:T(8,128)(2,1)S(1)}, u32[]{:S(2)}, u32[]{:S(2)}) collective-permute-start(bf16[3,256,1024]{1,2,0:T(8,128)(2,1)S(1)} %fusion.10), channel_id=1, source_target_pairs={{0,448},{64,0},{128,64},{192,128},{256,192},{320,256},{384,320},{4... | collective-permute-start | bytes 4718600 | tf_op jit(solution)/shard_map/ppermute | solution.py:17
  171.2 22.0 %copy-start.7 = (bf16[3,256,1024]{1,2,0:T(8,128)(2,1)}, bf16[3,256,1024]{1,2,0:T(8,128)(2,1)S(1)}, u32[]{:S(2)}) copy-start(bf16[3,256,1024]{1,2,0:T(8,128)(2,1)S(1)} %collective-permute-done.1) | copy-start | bytes 4718596
  171.2 21.2 %collective-permute-start.2 = (bf16[3,256,1024]{1,2,0:T(8,128)(2,1)S(1)}, bf16[3,256,1024]{1,2,0:T(8,128)(2,1)}, u32[]{:S(2)}, u32[]{:S(2)}) collective-permute-start(bf16[3,256,1024]{1,2,0:T(8,128)(2,1)S(1)} %collective-permute-done.1), channel_id=1, source_target_pairs={{0,64},{64,128},{128,192},{192,256},{256,320},{320,384},{384,448},... | collective-permute-start | bytes 4718600 | tf_op jit(solution)/shard_map/ppermute | solution.py:15
  171.2 1.2 copy-start.5
  172.4 20.9 %collective-permute-start.5 = (bf16[3,256,1024]{1,2,0:T(8,128)(2,1)S(1)}, bf16[3,256,1024]{1,2,0:T(8,128)(2,1)}, u32[]{:S(2)}, u32[]{:S(2)}) collective-permute-start(bf16[3,256,1024]{1,2,0:T(8,128)(2,1)S(1)} %collective-permute-done.4), channel_id=1, source_target_pairs={{0,448},{64,0},{128,64},{192,128},{256,192},{320,256},{384,320},{4... | collective-permute-start | bytes 4718600 | tf_op jit(solution)/shard_map/ppermute | solution.py:17
  192.4 21.4 %collective-permute-start.3 = (bf16[3,256,1024]{1,2,0:T(8,128)(2,1)}, bf16[3,256,1024]{1,2,0:T(8,128)(2,1)}, u32[]{:S(2)}, u32[]{:S(2)}) collective-permute-start(bf16[3,256,1024]{1,2,0:T(8,128)(2,1)} %collective-permute-done.2), channel_id=1, source_target_pairs={{0,64},{64,128},{128,192},{192,256},{256,320},{320,384},{384,448},... | collective-permute-start | bytes 4718600 | tf_op jit(solution)/shard_map/ppermute | solution.py:15
  193.3 25.6 %collective-permute-start.6 = (bf16[3,256,1024]{1,2,0:T(8,128)(2,1)}, bf16[3,256,1024]{1,2,0:T(8,128)(2,1)}, u32[]{:S(2)}, u32[]{:S(2)}) collective-permute-start(bf16[3,256,1024]{1,2,0:T(8,128)(2,1)} %collective-permute-done.5), channel_id=1, source_target_pairs={{0,448},{64,0},{128,64},{192,128},{256,192},{320,256},{384,320},{4... | collective-permute-start | bytes 4718600 | tf_op jit(solution)/shard_map/ppermute | solution.py:17
  196.5 20.4 %copy-start.8 = (bf16[3,256,1024]{1,2,0:T(8,128)(2,1)S(1)}, bf16[3,256,1024]{1,2,0:T(8,128)(2,1)}, u32[]{:S(2)}) copy-start(bf16[3,256,1024]{1,2,0:T(8,128)(2,1)} %copy-done.7) | copy-start | bytes 4718596
  215.3 2.0 copy-start.6
  232.0 16.4 %copy-start.9 = (f32[24,24]{1,0:T(8,128)S(1)}, f32[24,24]{1,0:T(8,128)}, u32[]{:S(2)}) copy-start(f32[24,24]{1,0:T(8,128)} %param.8) | copy-start | bytes 6916
  257.4 1.3 copy-start.4
  259.3 33.1 %collective-permute-start.7 = (bf16[3,256,1024]{2,1,0:T(8,128)(2,1)S(1)}, bf16[3,256,1024]{2,1,0:T(8,128)(2,1)S(1)}, u32[]{:S(2)}, u32[]{:S(2)}) collective-permute-start(bf16[3,256,1024]{2,1,0:T(8,128)(2,1)S(1)} %copy.17), channel_id=1, source_target_pairs={{0,1},{1,0},{2,3},{3,2},{4,5},{5,4},{6,7},{7,6},{8,9},{9,8},{10,11... | collective-permute-start | bytes 4718600 | tf_op jit(solution)/shard_map/ppermute | solution.py:23
  299.8 1.9 copy-start.2
  304.7 134.3 %collective-permute-start.8 = (bf16[3,512,1024]{2,1,0:T(8,128)(2,1)}, bf16[3,512,1024]{2,1,0:T(8,128)(2,1)}, u32[]{:S(2)}, u32[]{:S(2)}) collective-permute-start(bf16[3,512,1024]{2,1,0:T(8,128)(2,1)} %copy.20), channel_id=1, source_target_pairs={{0,2},{1,3},{2,0},{3,1},{4,6},{5,7},{6,4},{7,5},{8,10},{9,11},{10,... | collective-permute-start | bytes 9437192 | tf_op jit(solution)/shard_map/ppermute | solution.py:23
  309.0 134.6 %copy-start.3 = (bf16[3,512,1024]{2,0,1:T(4,128)(2,1)S(1)}, bf16[3,512,1024]{2,0,1:T(4,128)(2,1)}, u32[]{:S(2)}) copy-start(bf16[3,512,1024]{2,0,1:T(4,128)(2,1)} %copy-done.2) | copy-start | bytes 9437188
  443.6 9.4 %copy-start.10 = (bf16[3,256,1024]{2,1,0:T(8,128)(2,1)S(1)}, bf16[3,256,1024]{2,1,0:T(8,128)(2,1)}, u32[]{:S(2)}) copy-start(bf16[3,256,1024]{2,1,0:T(8,128)(2,1)} %param.7) | copy-start | bytes 4718596
  443.6 57.3 %copy-start.1 = (bf16[3,256,1024]{2,1,0:T(8,128)(2,1)S(1)}, bf16[3,256,1024]{2,1,0:T(8,128)(2,1)}, u32[]{:S(2)}) copy-start(bf16[3,256,1024]{2,1,0:T(8,128)(2,1)} %param.6) | copy-start | bytes 4718596
Sparse Core Ops, SparseCore 0:
  458.3 41.0 reduce-scatter.1
